TPU v7x, 256 devices: a whole 4x4x8 slice. The times are simulated.
256 devices in a mesh: pair: 32 (over y, x, core), lam: 8 (over z).
Axes of the slice: x: 4, y: 4, z: 8, core: 2. Of those that a mesh axis runs over, the one named last changes fastest.
Arguments:
- integrals: bfloat16 [32, 64, 4, 64, 1024], P('pair', 'lam'), may hold values from -0.119628906 to 0.119628906
- tile_pair: int32 [32, 64], P('pair', 'lam'), may hold values from 0 to 15, as said below
- tile_lam: int32 [32, 64], P('pair', 'lam'), may hold values from 0 to 15, as said below
- tile_count: int32 [32, 8], P('pair', 'lam'), may hold values from 1 to 8, as said below
- mu_index: int32 [2048], P('pair'), may hold values from 0 to 1023
- nu_index: int32 [2048], P('pair'), may hold values from 0 to 1023
- occupied_coef: bfloat16 [1024, 16], replicated, may hold values from -1.5 to 1.5
- virtual_coef: bfloat16 [1024, 1280], replicated, may hold values from -1.5 to 1.5
Outputs:
- orbital_integrals: float32 [16, 1280, 20480], P('lam', 'pair')
Inputs may be any that keep to these rules, and one draw needn't show every extreme that they name: On every device the live and dead slots name distinct pairs of (tile_pair, tile_lam); tile_pair lies in 0 to 15. On lam index l every slot's tile_lam lies in l * 2 to (l + 1) * 2 - 1. Slots from tile_count on are dead and their integrals are ignored; some device has all 8 slots live.
All inputs are finite; a program needn't handle non-finite values.
Results may differ from a plain program's by a relative error of at most 0.0049.
Values may be sent and summed in bfloat16 or wider, within the bound.
No kernel may reach another device: no remote copies, remote signals or barrier semaphores. Data moves between devices by JAX's collectives and lax.ppermute only.
A program may use at most 128 MiB of HBM per device.

v0:
```python
import jax
import jax.numpy as jnp
from jax import lax
from jax.sharding import PartitionSpec as P


def on_device(
    integrals, tile_pair, tile_lam, tile_count, mu_index, nu_index, occupied_coef, virtual_coef
):
    lam_count = lax.axis_size("lam")
    pair_count = lax.axis_size("pair")
    basis_count, occ_total = occupied_coef.shape
    vir_total = virtual_coef.shape[1]
    rows_here = mu_index.shape[0]
    occ_share = occ_total // lam_count
    vir_share = vir_total // pair_count
    tile_data = integrals[0]
    slot_count, tile_rows, tile_depth, _ = tile_data.shape
    block_count = rows_here // tile_rows
    pair_list = tile_pair[0]
    lam_list = tile_lam[0]
    live = jnp.arange(slot_count) < tile_count[0, 0]
    occ_blocks = occupied_coef.reshape(basis_count // tile_depth, tile_depth, occ_total)
    occ_slot = jnp.take(occ_blocks, lam_list, axis=0)
    occ_slot = jnp.where(live[:, None, None], occ_slot, jnp.zeros((), occ_slot.dtype))
    contrib = jnp.einsum("tmj,tkms->jtks", occ_slot, tile_data, preferred_element_type=jnp.float32)
    peak = jnp.maximum(jnp.max(jnp.abs(contrib)), 1e-30)
    exponent = jnp.clip(jnp.floor(jnp.log2(peak)), -100.0, 100.0)
    scale = jnp.exp2(13.0 - exponent)
    payload = (
        (contrib * scale)
        .astype(jnp.float16)
        .reshape(lam_count, occ_share, slot_count, tile_rows, basis_count)
    )
    hit = (pair_list[:, None] == jnp.arange(block_count)[None, :]) & live[:, None]
    info = jnp.zeros((slot_count, 128), jnp.float32)
    info = info.at[:, :block_count].set(hit.astype(jnp.float32))
    info = info.at[:, block_count].set(exponent)
    info = jnp.broadcast_to(
        info.astype(jnp.float16)[None, None, :, None, :],
        (lam_count, occ_share, slot_count, tile_rows, 128),
    )
    payload = jnp.concatenate([payload, info], axis=4)
    own_rows = jnp.zeros((2, pair_count, rows_here), jnp.float32)
    own_rows = lax.dynamic_update_index_in_dim(
        own_rows,
        jnp.stack([mu_index, nu_index]).astype(jnp.float32)[:, None],
        lax.axis_index("pair"),
        1,
    )
    both_index = lax.psum(own_rows, "pair").astype(jnp.int32).reshape(2, pair_count * rows_here)
    got = lax.all_to_all(payload, "lam", split_axis=0, concat_axis=0, tiled=True)
    got_info = got[:, 0, :, 0, basis_count:].astype(jnp.float32)
    unscale = jnp.exp2(got_info[:, 0, block_count] - 13.0)
    got_hit = got_info[:, :, :block_count] * unscale[:, None, None]
    own_half = jnp.einsum(
        "ptg,pjtks->jgks",
        got_hit,
        got[..., :basis_count].astype(jnp.float32),
        precision=lax.Precision.HIGHEST,
        preferred_element_type=jnp.float32,
    ).reshape(occ_share, rows_here, basis_count)
    half_low = own_half.astype(jnp.bfloat16).reshape(occ_share * rows_here, basis_count)
    mixed = jnp.dot(half_low, virtual_coef, preferred_element_type=jnp.float32)
    mixed = mixed.astype(jnp.bfloat16).reshape(occ_share, rows_here, pair_count, vir_share)
    received = lax.all_to_all(mixed, "pair", split_axis=2, concat_axis=1, tiled=True)
    total_rows = received.shape[1]
    mixed_rows = received.reshape(occ_share, total_rows, vir_share)
    occ_rows = jnp.take(occupied_coef, both_index[0], axis=0)
    vir_rows = jnp.take(virtual_coef, both_index[1], axis=0)
    scaled = (
        mixed_rows.astype(jnp.float32)[:, :, :, None]
        * occ_rows.astype(jnp.float32)[None, :, None, :]
    ).astype(jnp.bfloat16)
    result = jnp.einsum("qrbi,ra->qbia", scaled, vir_rows, preferred_element_type=jnp.float32)
    return result.reshape(occ_share, vir_share, occ_total * vir_total)


def solution(mesh):
    placed = (
        P("pair", "lam", None, None, None),
        P("pair", "lam"),
        P("pair", "lam"),
        P("pair", "lam"),
        P("pair"),
        P("pair"),
        P(),
        P(),
    )
    return jax.shard_map(
        on_device, mesh=mesh, in_specs=placed, out_specs=P("lam", "pair", None), check_vma=False
    )
```

profile of v0, /device:TPU:1, one launch (start us, length us, event | category | flops | bytes accessed | tf_op | source)
XLA Modules:
  0.0 209.2 jit_solution(5575800816990912734)
XLA Ops:
  0.0 0.0 copy-start
  0.0 0.7 compare_reduce_fusion.1
  0.7 0.6 compare_reduce_fusion
  2.0 0.7 fusion.28
  2.7 0.7 compare_and_fusion.2
  3.3 0.9 reshape.236
  4.2 0.6 gather_fusion
  4.8 0.0 copy-start.4
  4.8 4.9 %abs_reduce_fusion = (f32[]{:T(128)}, f32[8,16,4,1024]{3,1,2,0:T(8,128)}) fusion(bf16[1,8,4,64,1024]{4,3,2,1,0:T(8,128)(2,1)} %param.12, bf16[8,64,16]{1,2,0:T(8,128)(2,1)S(1)} %gather_fusion, pred[8]{0:T(512)(128)(4,1)S(1)} %get-tuple-element.33, pred[8]{0:T(512)(128)(4,1)S(1)} %get-tuple-element.34), kind=kOutput, calls=%fused_computation.15 | convolution fusion | flops 68173824 | bytes 6307860 | tf_op jit(solution)/shard_map/tmj,tkms->jtks/dot_general | solution.py:26
  10.4 0.0 copy-done.4
  10.4 0.8 convert_select_fusion
  11.8 1.9 fusion.11
  13.6 1.6 copy.45
  15.2 0.0 copy-start.2
  15.2 0.0 copy-start.3
  15.2 0.0 copy-start.1
  15.2 0.1 scatter.9
  15.4 2.6 %pad_maximum_fusion = f16[8,2,8,4,1152]{4,2,3,1,0:T(8,128)(2,1)} fusion(f16[8,2,8,4,128]{4,2,3,1,0:T(8,128)(2,1)S(1)} %broadcast_in_dim.64, f16[8,2,8,4,1024]{4,2,3,1,0:T(8,128)(2,1)} %bitcast.76), kind=kLoop, calls=%fused_computation.19 | loop fusion | flops 589824 | bytes 2359296 | tf_op jit(solution)/shard_map/concatenate | solution.py:43
  17.9 9.0 %all-to-all-start = ((f16[8,2,8,4,1152]{4,2,3,1,0:T(8,128)(2,1)}), f16[8,2,8,4,1152]{4,2,3,1,0:T(8,128)(2,1)}, u32[]{:S(2)}, u32[]{:S(2)}) async-start(f16[8,2,8,4,1152]{4,2,3,1,0:T(8,128)(2,1)} %pad_maximum_fusion), calls=%async_computation | async-start | bytes 2359296 | tf_op jit(solution)/shard_map/all_to_all | solution.py:52
  27.0 0.0 copy-done.2
  27.0 0.0 copy-done.3
  27.0 123.8 %psum.7 = f32[2,32,64]{2,1,0:T(8,128)S(1)} all-reduce(f32[2,32,64]{2,1,0:T(8,128)S(1)} %dynamic_update_slice.4), channel_id=1, replica_groups=mesh['pair'=32,'lam'=8] {'pair'}, use_global_device_ids=true, to_apply=%region_3.4 | all-reduce | flops 4096 | bytes 32768 | tf_op jit(solution)/shard_map/psum | solution.py:51
  150.9 0.1 squeeze.28
  150.9 0.1 squeeze.27
  151.0 0.0 copy-done.1
  151.0 0.2 copy.39
  151.2 0.1 squeeze.30
  151.3 6.2 %gather_fusion.1 = bf16[2048,16]{1,0:T(8,128)(2,1)S(1)} fusion(bf16[1024,16]{1,0:T(8,128)(2,1)S(1)} %copy.39, s32[2048]{0:T(1024)S(1)} %broadcast_clamp_fusion.1), kind=kCustom, calls=%fused_computation.1 | custom fusion | bytes 139264 | tf_op jit(solution)/shard_map/jit(_take)/gather | solution.py:69
  157.5 0.2 copy.40
  157.7 0.0 all-to-all-done
  157.8 0.7 fusion.20
  158.5 0.2 fusion.26
  158.7 2.2 %fusion.10 = bf16[2,16,4,1024]{3,1,2,0:T(8,128)(2,1)S(1)} fusion(f16[8,2,8,4,1152]{4,2,3,1,0:T(8,128)(2,1)} %all-to-all-done, f32[8,8,128]{2,1,0:T(8,128)S(1)} %fusion.20, f32[8]{0:T(128)S(1)} %fusion.26), kind=kOutput, calls=%fused_computation.20 | convolution fusion | flops 100795392 | bytes 1343520 | tf_op jit(solution)/shard_map/ptg,pjtks->jgks/dot_general | solution.py:56
  160.9 0.2 copy.36
  161.1 0.1 convert_element_type.79
  161.2 0.0 copy-done
  161.2 0.5 convolution_convert_fusion
  161.7 0.9 copy.37
  162.6 1.3 reshape.238
  163.9 1.1 reshape.272
  165.0 9.8 %all-to-all-start.1 = ((bf16[32,2,2560]{2,1,0:T(2,128)(2,1)}), bf16[32,2,2560]{2,1,0:T(2,128)(2,1)}, u32[]{:S(2)}, u32[]{:S(2)}) async-start(bf16[32,2,2560]{2,1,0:T(2,128)(2,1)} %reshape.272), calls=%async_computation.1 | async-start | bytes 655360 | tf_op jit(solution)/shard_map/all_to_all | solution.py:66
  174.9 0.1 squeeze.29
  174.9 9.8 %gather_fusion.2 = bf16[2048,1280]{1,0:T(8,128)(2,1)} fusion(bf16[1024,1280]{1,0:T(8,128)(2,1)S(1)} %copy-done, s32[2048]{0:T(1024)S(1)} %broadcast_clamp_fusion), kind=kCustom, calls=%fused_computation.2 | custom fusion | bytes 10493952 | tf_op jit(solution)/shard_map/jit(_take)/gather | solution.py:70
  184.8 0.0 all-to-all-done.1
  184.8 1.4 reshape.273
  186.2 0.5 convert_bitcast_fusion
  186.7 1.5 copy.38
  188.2 1.7 reshape.241
  189.9 11.6 %fusion = f32[2,40,16,1280]{3,2,1,0:T(8,128)} fusion(bf16[2048,1280]{1,0:T(8,128)(2,1)} %gather_fusion.2, f32[2048,16]{0,1:T(8,128)S(1)} %select_convert_fusion, f32[2,2048,40]{1,2,0:T(8,128)S(1)} %reshape.241, pred[2048]{0:T(1024)(128)(4,1)S(1)} %compare_and_fusion), kind=kOutput, calls=%fused_computation.4 | convolution fusion | flops 6718750720 | bytes 12584960 | tf_op jit(solution)/shard_map/qrbi,ra->qbia/dot_general | solution.py:75
  201.5 7.7 %reshape.239 = f32[2,40,20480]{2,1,0:T(8,128)} reshape(f32[2,40,16,1280]{3,2,1,0:T(8,128)} %fusion) | data formatting | bytes 13107200 | tf_op jit(solution)/shard_map/reshape | solution.py:76
  (18 shorter events, 0.2 us)
Async XLA Ops:
  0.0 161.2 %copy-start = (bf16[1024,1280]{1,0:T(8,128)(2,1)S(1)}, bf16[1024,1280]{1,0:T(8,128)(2,1)}, u32[]{:S(2)}) copy-start(bf16[1024,1280]{1,0:T(8,128)(2,1)} %param.19) | copy-start | bytes 7864324
  4.8 5.6 %copy-start.4 = (s32[1,8]{1,0:T(1,128)S(1)}, s32[1,8]{1,0:T(1,128)}, u32[]{:S(2)}) copy-start(s32[1,8]{1,0:T(1,128)} %param.13) | copy-start | bytes 100
  15.2 11.7 %copy-start.2 = (s32[64]{0:T(128)S(1)}, s32[64]{0:T(128)}, u32[]{:S(2)}) copy-start(s32[64]{0:T(128)} %param.17) | copy-start | bytes 772
  15.2 11.7 %copy-start.3 = (s32[64]{0:T(128)S(1)}, s32[64]{0:T(128)}, u32[]{:S(2)}) copy-start(s32[64]{0:T(128)} %param.16) | copy-start | bytes 772
  15.2 135.8 %copy-start.1 = (bf16[1024,16]{0,1:T(8,128)(2,1)S(1)}, bf16[1024,16]{0,1:T(8,128)(2,1)}, u32[]{:S(2)}) copy-start(bf16[1024,16]{0,1:T(8,128)(2,1)} %param.18) | copy-start | bytes 98308
  17.9 139.8 %all-to-all-start = ((f16[8,2,8,4,1152]{4,2,3,1,0:T(8,128)(2,1)}), f16[8,2,8,4,1152]{4,2,3,1,0:T(8,128)(2,1)}, u32[]{:S(2)}, u32[]{:S(2)}) async-start(f16[8,2,8,4,1152]{4,2,3,1,0:T(8,128)(2,1)} %pad_maximum_fusion), calls=%async_computation | async-start | bytes 2359296 | tf_op jit(solution)/shard_map/all_to_all | solution.py:52
  165.0 19.8 %all-to-all-start.1 = ((bf16[32,2,2560]{2,1,0:T(2,128)(2,1)}), bf16[32,2,2560]{2,1,0:T(2,128)(2,1)}, u32[]{:S(2)}, u32[]{:S(2)}) async-start(bf16[32,2,2560]{2,1,0:T(2,128)(2,1)} %reshape.272), calls=%async_computation.1 | async-start | bytes 655360 | tf_op jit(solution)/shard_map/all_to_all | solution.py:66
where the time goes:
time: 210 us; the launch traced here: 209 us
  blocking collectives  124 us (59%)
  local copies, waits for them, and re-layouts  35.8 us (17%)
  matrix products  19.2 us (9%)
  starting transfers between devices  18.8 us (9%)
  other arithmetic  9.33 us (4%)
  between operations  2.18 us (1%)
    psum x1, blocking collectives, on_device(): lax.psum(own_rows, 'pair').astype(jnp.int32)  124 us
    dot_general x1, matrix products, on_device(): jnp.einsum('qrbi,ra->qbia', scaled, vir_rows, preferred_element_type=jnp....  11.6 us
    gather x1, local copies, waits for them, and re-layouts, on_device(): vir_rows = jnp.take(virtual_coef, both_index[1], axis=0)  9.85 us
    all_to_all x1, starting transfers between devices, on_device(): lax.all_to_all(mixed, 'pair', split_axis=2, concat_axis=1, tiled=True)  9.83 us
    all_to_all x1, starting transfers between devices, on_device(): lax.all_to_all(payload, 'lam', split_axis=0, concat_axis=0, tiled=True)  9.01 us
    reshape x1, local copies, waits for them, and re-layouts, on_device(): return result.reshape(occ_share, vir_share, occ_total * vir_total)  7.69 us
    gather x2, local copies, waits for them, and re-layouts, on_device(): occ_rows = jnp.take(occupied_coef, both_index[0], axis=0)  6.36 us
    dot_general x1, matrix products, on_device(): jnp.einsum('tmj,tkms->jtks', occ_slot, tile_data, preferred_element_type=...  4.87 us
  transfers between devices with their start and end apart: 2, of which 0 were waited for; matrix products, arithmetic and copies ran while one was open for 8% of the time, Pallas kernels for 0%

commit v1 on v0

--- a/solution.py
+++ b/solution.py
@@ -48,7 +48,11 @@
         lax.axis_index("pair"),
         1,
     )
-    both_index = lax.psum(own_rows, "pair").astype(jnp.int32).reshape(2, pair_count * rows_here)
+    both_index = (
+        jnp.sum(lax.all_gather(own_rows, "pair"), axis=0)
+        .astype(jnp.int32)
+        .reshape(2, pair_count * rows_here)
+    )
     got = lax.all_to_all(payload, "lam", split_axis=0, concat_axis=0, tiled=True)
     got_info = got[:, 0, :, 0, basis_count:].astype(jnp.float32)
     unscale = jnp.exp2(got_info[:, 0, block_count] - 13.0)

time: 210 us -> 111 us (0.53)
  blocking collectives: 124 us -> 28.3 us
  starting transfers between devices: 18.8 us -> 14.2 us
    psum x1 -> x0, blocking collectives: 124 us -> none  [on_device(): lax.psum(own_rows, 'pair').astype(jnp.int32)]
    all_gather x0 -> x1, blocking collectives: none -> 28.3 us  [on_device(): lax.all_gather(own_rows, 'pair')]
    all_to_all x1, starting transfers between devices: 9.83 us -> 5.21 us  [on_device(): lax.all_to_all(mixed, 'pair', split_axis=2, concat_axis=1, tiled=True)]
  transfers between devices with their start and end apart: 2 -> 2, of which waited for: 0 -> 0; matrix products, arithmetic and copies ran while one was open for 8% -> 16% of each run, Pallas kernels for 0% -> 0%
where the time goes in v1:
time: 111 us; the launch traced here: 110 us
  local copies, waits for them, and re-layouts  35.8 us (32%)
  blocking collectives  28.3 us (25%)
  matrix products  19.2 us (17%)
  starting transfers between devices  14.2 us (13%)
  other arithmetic  10.7 us (10%)
  between operations  2.19 us (2%)
    all_gather x1, blocking collectives, on_device(): lax.all_gather(own_rows, 'pair')  28.3 us
    dot_general x1, matrix products, on_device(): jnp.einsum('qrbi,ra->qbia', scaled, vir_rows, preferred_element_type=jnp....  11.6 us
    gather x1, local copies, waits for them, and re-layouts, on_device(): vir_rows = jnp.take(virtual_coef, both_index[1], axis=0)  9.85 us
    all_to_all x1, starting transfers between devices, on_device(): lax.all_to_all(payload, 'lam', split_axis=0, concat_axis=0, tiled=True)  9.01 us
    reshape x1, local copies, waits for them, and re-layouts, on_device(): return result.reshape(occ_share, vir_share, occ_total * vir_total)  7.69 us
    gather x2, local copies, waits for them, and re-layouts, on_device(): occ_rows = jnp.take(occupied_coef, both_index[0], axis=0)  6.36 us
    all_to_all x1, starting transfers between devices, on_device(): lax.all_to_all(mixed, 'pair', split_axis=2, concat_axis=1, tiled=True)  5.21 us
    dot_general x1, matrix products, on_device(): jnp.einsum('tmj,tkms->jtks', occ_slot, tile_data, preferred_element_type=...  4.87 us
  transfers between devices with their start and end apart: 2, of which 0 were waited for; matrix products, arithmetic and copies ran while one was open for 16% of the time, Pallas kernels for 0%

profile of v1, /device:TPU:1, one launch (start us, length us, event | category | flops | bytes accessed | tf_op | source)
XLA Modules:
  0.0 110.3 jit_solution(9049036390914535623)
XLA Ops:
  0.0 0.0 copy-start
  0.0 0.7 compare_reduce_fusion.1
  0.7 0.6 compare_reduce_fusion
  2.0 0.7 fusion.28
  2.7 0.7 compare_and_fusion.2
  3.3 0.9 reshape.242
  4.2 0.6 gather_fusion
  4.8 0.0 copy-start.4
  4.8 4.9 %abs_reduce_fusion = (f32[]{:T(128)}, f32[8,16,4,1024]{3,1,2,0:T(8,128)}) fusion(bf16[1,8,4,64,1024]{4,3,2,1,0:T(8,128)(2,1)} %param.12, bf16[8,64,16]{1,2,0:T(8,128)(2,1)S(1)} %gather_fusion, pred[8]{0:T(512)(128)(4,1)S(1)} %get-tuple-element.33, pred[8]{0:T(512)(128)(4,1)S(1)} %get-tuple-element.34), kind=kOutput, calls=%fused_computation.15 | convolution fusion | flops 68173824 | bytes 6307860 | tf_op jit(solution)/shard_map/tmj,tkms->jtks/dot_general | solution.py:26
  10.4 0.0 copy-done.4
  10.4 0.8 convert_select_fusion
  11.8 1.9 %fusion.11 = f16[16,8,4,1024]{3,0,2,1:T(8,128)(2,1)S(1)} fusion(f32[8,16,4,1024]{3,1,2,0:T(8,128)} %get-tuple-element.32, f32[]{:T(128)S(6)} %exp2.15), kind=kLoop, calls=%fused_computation.21 | loop fusion | flops 1048576 | bytes 3145732 | tf_op jit(solution)/shard_map/convert_element_type | solution.py:32
  13.6 1.6 %copy.45 = f16[16,8,4,1024]{3,1,2,0:T(8,128)(2,1)} copy(f16[16,8,4,1024]{3,0,2,1:T(8,128)(2,1)S(1)} %fusion.11) | data formatting | bytes 2097152 | tf_op jit(solution)/shard_map/reshape | solution.py:33
  15.2 0.0 copy-start.2
  15.2 0.0 copy-start.3
  15.2 0.1 scatter.9
  15.4 0.0 copy-start.1
  15.4 2.6 %pad_maximum_fusion = f16[8,2,8,4,1152]{4,2,3,1,0:T(8,128)(2,1)} fusion(f16[8,2,8,4,128]{4,2,3,1,0:T(8,128)(2,1)S(1)} %broadcast_in_dim.64, f16[8,2,8,4,1024]{4,2,3,1,0:T(8,128)(2,1)} %bitcast.76), kind=kLoop, calls=%fused_computation.19 | loop fusion | flops 589824 | bytes 2359296 | tf_op jit(solution)/shard_map/concatenate | solution.py:43
  17.9 9.0 %all-to-all-start = ((f16[8,2,8,4,1152]{4,2,3,1,0:T(8,128)(2,1)}), f16[8,2,8,4,1152]{4,2,3,1,0:T(8,128)(2,1)}, u32[]{:S(2)}, u32[]{:S(2)}) async-start(f16[8,2,8,4,1152]{4,2,3,1,0:T(8,128)(2,1)} %pad_maximum_fusion), calls=%async_computation | async-start | bytes 2359296 | tf_op jit(solution)/shard_map/all_to_all | solution.py:56
  26.9 0.0 copy-done.2
  26.9 0.0 copy-done.3
  27.0 28.3 %all_gather.4 = f32[32,2,32,64]{3,2,1,0:T(8,128)} all-gather(f32[1,2,32,64]{3,2,1,0:T(8,128)S(1)} %dynamic_update_slice.5), channel_id=1, replica_groups=mesh['pair'=32,'lam'=8] {'pair'}, dimensions={0}, use_global_device_ids=true | all-gather | bytes 540672 | tf_op jit(solution)/shard_map/all_gather | solution.py:52
  55.3 0.0 copy-done.1
  55.3 0.2 copy.39
  55.5 1.3 %reduce_sum.9 = f32[2,32,64]{2,1,0:T(8,128)S(1)} reduce(f32[32,2,32,64]{3,2,1,0:T(8,128)} %all_gather.4, f32[]{:T(128)} %constant.125.clone.1), dimensions={0}, to_apply=%region_3.4 | reduce | flops 126976 | bytes 540676 | tf_op jit(solution)/shard_map/reduce_sum | solution.py:52
  56.8 0.1 squeeze.28
  56.9 0.1 squeeze.27
  57.0 0.1 squeeze.30
  57.1 6.2 %gather_fusion.1 = bf16[2048,16]{1,0:T(8,128)(2,1)S(1)} fusion(bf16[1024,16]{1,0:T(8,128)(2,1)S(1)} %copy.39, s32[2048]{0:T(1024)S(1)} %broadcast_clamp_fusion.1), kind=kCustom, calls=%fused_computation.1 | custom fusion | bytes 139264 | tf_op jit(solution)/shard_map/jit(_take)/gather | solution.py:73
  63.3 0.2 copy.40
  63.5 0.0 all-to-all-done
  63.5 0.7 fusion.20
  64.3 0.2 fusion.26
  64.5 2.2 %fusion.10 = bf16[2,16,4,1024]{3,1,2,0:T(8,128)(2,1)S(1)} fusion(f16[8,2,8,4,1152]{4,2,3,1,0:T(8,128)(2,1)} %all-to-all-done, f32[8,8,128]{2,1,0:T(8,128)S(1)} %fusion.20, f32[8]{0:T(128)S(1)} %fusion.26), kind=kOutput, calls=%fused_computation.20 | convolution fusion | flops 100795392 | bytes 1343520 | tf_op jit(solution)/shard_map/ptg,pjtks->jgks/dot_general | solution.py:60
  66.7 0.2 copy.36
  66.9 0.1 convert_element_type.80
  67.0 0.0 copy-done
  67.0 0.5 convolution_convert_fusion
  67.5 0.9 copy.37
  68.4 1.3 %reshape.244 = bf16[2,64,32,40]{1,0,3,2:T(2,128)(2,1)S(1)} reshape(bf16[128,1280]{0,1:T(8,128)(2,1)} %copy.37) | data formatting | bytes 655360 | tf_op jit(solution)/shard_map/reshape | solution.py:69
  69.7 1.1 %reshape.278 = bf16[32,2,2560]{2,1,0:T(2,128)(2,1)} reshape(bf16[32,40,2,64]{3,2,1,0:T(2,128)(2,1)S(1)} %bitcast.77) | data formatting | bytes 655360
  70.8 5.2 %all-to-all-start.1 = ((bf16[32,2,2560]{2,1,0:T(2,128)(2,1)}), bf16[32,2,2560]{2,1,0:T(2,128)(2,1)}, u32[]{:S(2)}, u32[]{:S(2)}) async-start(bf16[32,2,2560]{2,1,0:T(2,128)(2,1)} %reshape.278), calls=%async_computation.1 | async-start | bytes 655360 | tf_op jit(solution)/shard_map/all_to_all | solution.py:70
  76.1 0.1 squeeze.29
  76.1 9.8 %gather_fusion.2 = bf16[2048,1280]{1,0:T(8,128)(2,1)} fusion(bf16[1024,1280]{1,0:T(8,128)(2,1)S(1)} %copy-done, s32[2048]{0:T(1024)S(1)} %broadcast_clamp_fusion), kind=kCustom, calls=%fused_computation.2 | custom fusion | bytes 10493952 | tf_op jit(solution)/shard_map/jit(_take)/gather | solution.py:74
  86.0 0.0 all-to-all-done.1
  86.0 1.4 %reshape.279 = bf16[32,40,2,64]{3,2,1,0:T(2,128)(2,1)S(1)} reshape(bf16[32,2,2560]{2,1,0:T(2,128)(2,1)} %all-to-all-done.1) | data formatting | bytes 655360
  87.4 0.5 convert_bitcast_fusion
  87.9 1.5 %copy.38 = f32[2,32,64,1,40]{2,1,4,0,3:T(8,128)} copy(f32[2,32,64,1,40]{2,0,4,1,3:T(2,128)S(1)} %convert_bitcast_fusion) | data formatting | bytes 1310720 | tf_op jit(solution)/shard_map/convert_element_type | solution.py:76
  89.3 1.7 %reshape.247 = f32[2,2048,40]{1,2,0:T(8,128)S(1)} reshape(f32[2,32,64,1,40]{2,1,4,0,3:T(8,128)} %copy.38) | data formatting | bytes 1310720 | tf_op jit(solution)/shard_map/convert_element_type | solution.py:76
  91.1 11.6 %fusion = f32[2,40,16,1280]{3,2,1,0:T(8,128)} fusion(bf16[2048,1280]{1,0:T(8,128)(2,1)} %gather_fusion.2, f32[2048,16]{0,1:T(8,128)S(1)} %select_convert_fusion, f32[2,2048,40]{1,2,0:T(8,128)S(1)} %reshape.247, pred[2048]{0:T(1024)(128)(4,1)S(1)} %compare_and_fusion), kind=kOutput, calls=%fused_computation.4 | convolution fusion | flops 6718750720 | bytes 12584960 | tf_op jit(solution)/shard_map/qrbi,ra->qbia/dot_general | solution.py:79
  102.6 7.7 %reshape.245 = f32[2,40,20480]{2,1,0:T(8,128)} reshape(f32[2,40,16,1280]{3,2,1,0:T(8,128)} %fusion) | data formatting | bytes 13107200 | tf_op jit(solution)/shard_map/reshape | solution.py:80
  (18 shorter events, 0.2 us)
Async XLA Ops:
  0.0 67.0 %copy-start = (bf16[1024,1280]{1,0:T(8,128)(2,1)S(1)}, bf16[1024,1280]{1,0:T(8,128)(2,1)}, u32[]{:S(2)}) copy-start(bf16[1024,1280]{1,0:T(8,128)(2,1)} %param.19) | copy-start | bytes 7864324
  4.8 5.6 %copy-start.4 = (s32[1,8]{1,0:T(1,128)S(1)}, s32[1,8]{1,0:T(1,128)}, u32[]{:S(2)}) copy-start(s32[1,8]{1,0:T(1,128)} %param.13) | copy-start | bytes 100
  15.2 11.7 %copy-start.2 = (s32[64]{0:T(128)S(1)}, s32[64]{0:T(128)}, u32[]{:S(2)}) copy-start(s32[64]{0:T(128)} %param.17) | copy-start | bytes 772
  15.2 11.7 %copy-start.3 = (s32[64]{0:T(128)S(1)}, s32[64]{0:T(128)}, u32[]{:S(2)}) copy-start(s32[64]{0:T(128)} %param.16) | copy-start | bytes 772
  15.4 40.0 %copy-start.1 = (bf16[1024,16]{0,1:T(8,128)(2,1)S(1)}, bf16[1024,16]{0,1:T(8,128)(2,1)}, u32[]{:S(2)}) copy-start(bf16[1024,16]{0,1:T(8,128)(2,1)} %param.18) | copy-start | bytes 98308
  17.9 45.6 %all-to-all-start = ((f16[8,2,8,4,1152]{4,2,3,1,0:T(8,128)(2,1)}), f16[8,2,8,4,1152]{4,2,3,1,0:T(8,128)(2,1)}, u32[]{:S(2)}, u32[]{:S(2)}) async-start(f16[8,2,8,4,1152]{4,2,3,1,0:T(8,128)(2,1)} %pad_maximum_fusion), calls=%async_computation | async-start | bytes 2359296 | tf_op jit(solution)/shard_map/all_to_all | solution.py:56
  70.8 15.2 %all-to-all-start.1 = ((bf16[32,2,2560]{2,1,0:T(2,128)(2,1)}), bf16[32,2,2560]{2,1,0:T(2,128)(2,1)}, u32[]{:S(2)}, u32[]{:S(2)}) async-start(bf16[32,2,2560]{2,1,0:T(2,128)(2,1)} %reshape.278), calls=%async_computation.1 | async-start | bytes 655360 | tf_op jit(solution)/shard_map/all_to_all | solution.py:70
